TPU v7x, 32 devices: a whole 2x2x4 slice. The times are simulated.
32 devices in a mesh: groups: 2 (over x), wide: 16 (over z, y, core).
Axes of the slice: x: 2, y: 2, z: 4, core: 2. Of those that a mesh axis runs over, the one named last changes fastest.
Arguments:
- retarded_tiles: bfloat16 [32, 16, 2, 128, 128], P(('groups', 'wide')), parts along dimension 0, may hold values from -0.0625 to 0.0625
- tile_lags: int32 [32, 16, 2], P(('groups', 'wide')), parts along dimension 0, may hold values from 1 to 4, as said below
- block_owner: int32 [32], P('groups'), parts along dimension 0, may hold values from 0 to 15, each once
- later_current: bfloat16 [4, 4096, 128], P(None, ('groups', 'wide')), parts along dimension 1, may hold values from -6 to 6
- excitation: float32 [3, 4096, 128], P(None, ('groups', 'wide')), parts along dimension 1, may hold values from -6 to 6
- inverse_blocks: float32 [32, 128, 128], P(('groups', 'wide')), parts along dimension 0, may hold values from -0.5 to 0.5
Outputs:
- adjoint_current: float32 [3, 4096, 128], P(None, ('groups', 'wide')), parts along dimension 1
There are 2 independent parts, one for each index of `groups`. A program takes and returns all parts, laid end to end along the dimension named above; each array names one. Nothing has to cross between parts.
Inputs may be any that keep to these rules, and one draw needn't show every extreme that they name: `tile_lags`: the two slots of every tile name different lags. `block_owner`: each edge block is named once.
All inputs are finite; a program needn't handle non-finite values.
Results may differ from a plain program's by a relative error of at most 0.003.
Values may be sent and summed in bfloat16 or wider, within the bound.
No kernel may reach another device: no remote copies, remote signals or barrier semaphores. Data moves between devices by JAX's collectives and lax.ppermute only.
A program may use at most 128 MiB of HBM per device.

v0:
```python
import jax
import jax.numpy as jnp
from jax import lax
from jax.sharding import PartitionSpec as P


def per_device(retarded_tiles, tile_lags, block_owner, later_current, excitation, inverse_blocks):
    tile_size = retarded_tiles.shape[-1]
    pulses = later_current.shape[-1]
    lag_count = later_current.shape[0]
    step_count = excitation.shape[0]
    column_order = jnp.argsort(block_owner)
    local_tiles = jnp.take(retarded_tiles[0], column_order, axis=0)
    local_lags = jnp.take(tile_lags[0], column_order, axis=0)
    inverse = inverse_blocks[0]
    results = [None] * step_count
    later = lax.all_gather(later_current, "wide", axis=1, tiled=True)
    history = {}
    for offset in range(lag_count):
        history[step_count + offset] = later[offset].reshape(-1, tile_size, pulses)
    for moment in range(step_count - 1, -1, -1):
        chosen = jnp.zeros(local_lags.shape + (tile_size, pulses), jnp.bfloat16)
        for delay in range(1, lag_count + 1):
            chosen = jnp.where(
                (local_lags == delay)[:, :, None, None], history[moment + delay][:, None], chosen
            )
        retarded = jnp.einsum(
            "jspq,jspr->qr", local_tiles, chosen, preferred_element_type=jnp.float32
        )
        source = excitation[moment] - retarded
        current = jnp.dot(
            inverse.T, source, precision=lax.Precision.HIGHEST, preferred_element_type=jnp.float32
        )
        results[moment] = current
        if moment > 0:
            rounded = current.astype(jnp.bfloat16)[None]
            history[moment] = lax.all_gather(rounded, "wide", axis=0, tiled=True)
    return jnp.stack(results)


def solution(mesh):
    in_specs = (
        P(("groups", "wide"), None, None, None, None),
        P(("groups", "wide"), None, None),
        P("groups"),
        P(None, ("groups", "wide"), None),
        P(None, ("groups", "wide"), None),
        P(("groups", "wide"), None, None),
    )
    out_specs = P(None, ("groups", "wide"), None)
    return jax.shard_map(
        per_device, mesh=mesh, in_specs=in_specs, out_specs=out_specs, check_vma=False
    )
```

profile of v0, /device:TPU:0, one launch (start us, length us, event | category | flops | bytes accessed | tf_op | source)
XLA Modules:
  0.0 111.3 jit_solution(3623664762194302780)
XLA Ops:
  6.5 0.0 copy-start
  6.5 0.0 all-gather.4.cloned.1.call-start
  6.5 0.7 all-gather.4.cloned.1.call-update
  7.3 0.8 copy.7
  8.0 1.9 %sort.17 = (s32[16]{0:T(128)}, s32[16]{0:T(128)S(1)}) sort(s32[16]{0:T(128)} %param.8, s32[16]{0:T(128)S(1)} %iota.4), dimensions={0}, to_apply=%region_0.0 | sort | flops 64 | bytes 256 | tf_op jit(solution)/shard_map/jit(argsort)/sort | solution.py:12
  9.9 0.6 gather_fusion.1
  10.5 0.0 copy-done
  10.5 0.7 gather_fusion
  11.3 0.1 select_compare_fusion.3
  11.4 42.4 %all-gather.4.cloned.1.call-done = bf16[4,2048,128]{2,1,0:T(8,128)(2,1)} async-done(((bf16[4,128,128]{2,1,0:T(8,128)(2,1)}), bf16[4,2048,128]{2,1,0:T(8,128)(2,1)}) %all-gather.4.cloned.1.call-update) | async-done | bytes 2097168 | tf_op jit(solution)/shard_map/all_gather | solution.py:17
  53.7 1.7 %fusion.50 = (bf16[1,2048,128]{2,1,0:T(8,128)(2,1)S(1)}, bf16[1,2048,128]{2,1,0:T(8,128)(2,1)S(1)}, bf16[1,2048,128]{2,1,0:T(8,128)(2,1)S(1)}, bf16[1,2048,128]{2,1,0:T(8,128)(2,1)S(1)}) fusion(bf16[4,2048,128]{2,1,0:T(8,128)(2,1)} %all-gather.4.cloned.1.call-done), kind=kLoop, calls=%fused_computation.67 | loop fusion | bytes 4194304 | tf_op jit(solution)/shard_map/slice | solution.py:20
  55.4 0.0 copy-start.2
  55.4 0.0 copy-start.3
  55.4 0.0 copy-start.4
  55.4 0.0 copy-start.1
  55.4 1.9 %fusion = f32[128,128]{1,0:T(8,128)S(1)} fusion(pred[16,2]{1,0:T(8,128)(4,1)S(1)} %get-tuple-element.14, pred[16,2]{1,0:T(8,128)(4,1)S(1)} %get-tuple-element.13, pred[16,2]{1,0:T(8,128)(4,1)S(1)} %get-tuple-element.12, pred[16,2]{1,0:T(8,128)(4,1)S(1)} %get-tuple-element.11, bf16[16,128,128]{2,1,0:T(8,128)(2,1)S(1)} %bitcast.68, ...), kind=kOutput, calls=%fused_computation.6 | convolution fusion | flops 136855552 | bytes 3276944 | tf_op jit(solution)/shard_map/jspq,jspr->qr/dot_general | solution.py:27
  57.3 0.0 copy-done.2
  57.3 0.0 copy-done.3
  57.4 0.0 copy-done.4
  57.4 0.0 copy-done.1
  57.4 0.3 bitcast_convert_fusion.1
  57.7 20.6 %all-gather = bf16[2048,128]{0,1:T(8,128)(2,1)S(1)} all-gather(bf16[128,128]{0,1:T(8,128)(2,1)S(1)} %get-tuple-element.15), channel_id=2, replica_groups=mesh['groups'=2,'wide'=16] {'wide'}, dimensions={0}, use_global_device_ids=true | all-gather | bytes 557056 | tf_op jit(solution)/shard_map/all_gather | solution.py:37
  78.3 0.3 copy.14
  78.6 2.3 %fusion.1 = f32[128,128]{1,0:T(8,128)S(1)} fusion(pred[16,2]{1,0:T(8,128)(4,1)S(1)} %get-tuple-element.14, pred[16,2]{1,0:T(8,128)(4,1)S(1)} %get-tuple-element.13, pred[16,2]{1,0:T(8,128)(4,1)S(1)} %get-tuple-element.12, pred[16,2]{1,0:T(8,128)(4,1)S(1)} %get-tuple-element.11, bf16[16,128,128]{2,1,0:T(8,128)(2,1)S(1)} %bitcast.59, ...), kind=kOutput, calls=%fused_computation.7 | convolution fusion | flops 136855552 | bytes 3276944 | tf_op jit(solution)/shard_map/jspq,jspr->qr/dot_general | solution.py:27
  80.8 0.3 bitcast_convert_fusion
  81.1 18.9 %all-gather.1 = bf16[2048,128]{0,1:T(8,128)(2,1)S(1)} all-gather(bf16[128,128]{0,1:T(8,128)(2,1)S(1)} %get-tuple-element.17), channel_id=3, replica_groups=mesh['groups'=2,'wide'=16] {'wide'}, dimensions={0}, use_global_device_ids=true | all-gather | bytes 557056 | tf_op jit(solution)/shard_map/all_gather | solution.py:37
  100.0 1.0 copy.15
  101.0 2.3 %fusion.2 = f32[128,128]{1,0:T(8,128)S(1)} fusion(pred[16,2]{1,0:T(8,128)(4,1)S(1)} %get-tuple-element.14, pred[16,2]{1,0:T(8,128)(4,1)S(1)} %get-tuple-element.13, pred[16,2]{1,0:T(8,128)(4,1)S(1)} %get-tuple-element.12, pred[16,2]{1,0:T(8,128)(4,1)S(1)} %get-tuple-element.11, bf16[16,128,128]{2,1,0:T(8,128)(2,1)} %bitcast.61, ...), kind=kOutput, calls=%fused_computation.8 | convolution fusion | flops 136855552 | bytes 3276944 | tf_op jit(solution)/shard_map/jspq,jspr->qr/dot_general | solution.py:27
  103.3 0.3 convolution_bitcast_fusion
  103.6 0.8 copy.10
  (5 shorter events, 0.0 us)
Async XLA Ops:
  6.5 4.0 %copy-start = (bf16[1,16,2,128,128]{4,3,2,1,0:T(8,128)(2,1)S(1)}, bf16[1,16,2,128,128]{4,3,2,1,0:T(8,128)(2,1)}, u32[]{:S(2)}) copy-start(bf16[1,16,2,128,128]{4,3,2,1,0:T(8,128)(2,1)} %param.6) | copy-start | bytes 3145732
  6.5 47.2 %all-gather.4.cloned.1.call-start = ((), (), s32[]{:S(2)}) async-start(), calls=%async_computation | async-start | bytes 2228224 | tf_op jit(solution)/shard_map/all_gather | solution.py:17
  55.4 2.0 %copy-start.2 = (bf16[1,2048,128]{2,1,0:T(8,128)(2,1)}, bf16[1,2048,128]{2,1,0:T(8,128)(2,1)S(1)}, u32[]{:S(2)}) copy-start(bf16[1,2048,128]{2,1,0:T(8,128)(2,1)S(1)} %get-tuple-element.7) | copy-start | bytes 1572868
  55.4 2.0 %copy-start.3 = (bf16[1,2048,128]{2,1,0:T(8,128)(2,1)}, bf16[1,2048,128]{2,1,0:T(8,128)(2,1)S(1)}, u32[]{:S(2)}) copy-start(bf16[1,2048,128]{2,1,0:T(8,128)(2,1)S(1)} %get-tuple-element.10) | copy-start | bytes 1572868
  55.4 2.0 %copy-start.4 = (bf16[1,2048,128]{2,1,0:T(8,128)(2,1)}, bf16[1,2048,128]{2,1,0:T(8,128)(2,1)S(1)}, u32[]{:S(2)}) copy-start(bf16[1,2048,128]{2,1,0:T(8,128)(2,1)S(1)} %get-tuple-element.8) | copy-start | bytes 1572868
  55.4 2.0 %copy-start.1 = (f32[1,128,128]{2,1,0:T(8,128)S(1)}, f32[1,128,128]{2,1,0:T(8,128)}, u32[]{:S(2)}) copy-start(f32[1,128,128]{2,1,0:T(8,128)} %param.11) | copy-start | bytes 196612
Sparse Core Ops, SparseCore 0:
  9.5 44.1 all-gather.3
where the time goes:
time: 112 us; the launch traced here: 111 us
  waiting for transfers between devices  43.1 us (38%)
  blocking collectives  39.5 us (35%)
  between operations  13.5 us (12%)
  matrix products  7.31 us (7%)
  local copies, waits for them, and re-layouts  5.84 us (5%)
  other arithmetic  2.01 us (2%)
    all_gather x1, waiting for transfers between devices, per_device(): later = lax.all_gather(later_current, 'wide', axis=1, tiled=True)  42.4 us
    all_gather x2, blocking collectives, per_device(): history[moment] = lax.all_gather(rounded, 'wide', axis=0, tiled=True)  39.5 us
    dot_general x3, matrix products, per_device(): jnp.einsum('jspq,jspr->qr', local_tiles, chosen, preferred_element_type=j...  6.46 us
  transfers between devices with their start and end apart: 1, of which 1 were waited for; matrix products, arithmetic and copies ran while one was open for 4% of the time, Pallas kernels for 0%

commit v1 on v0

--- a/solution.py
+++ b/solution.py
@@ -2,6 +2,22 @@
 import jax.numpy as jnp
 from jax import lax
 from jax.sharding import PartitionSpec as P
+
+
+def collect(x, axis, dim):
+    ways, here, step = (lax.axis_size(axis), lax.axis_index(axis), x.shape[dim])
+    lengths = [n * ways if d == dim else n for d, n in enumerate(x.shape)]
+    full = lax.dynamic_update_slice_in_dim(jnp.zeros(lengths, x.dtype), x, here * step, axis=dim)
+    going_up = going_down = x
+    for far in range(1, ways // 2 + 1):
+        going_up = lax.ppermute(going_up, axis, [(d, (d + 1) % ways) for d in range(ways)])
+        full = lax.dynamic_update_slice_in_dim(full, going_up, (here - far) % ways * step, axis=dim)
+        if 2 * far < ways:
+            going_down = lax.ppermute(going_down, axis, [(d, (d - 1) % ways) for d in range(ways)])
+            full = lax.dynamic_update_slice_in_dim(
+                full, going_down, (here + far) % ways * step, axis=dim
+            )
+    return full
 
 
 def per_device(retarded_tiles, tile_lags, block_owner, later_current, excitation, inverse_blocks):
@@ -34,7 +50,7 @@
         results[moment] = current
         if moment > 0:
             rounded = current.astype(jnp.bfloat16)[None]
-            history[moment] = lax.all_gather(rounded, "wide", axis=0, tiled=True)
+            history[moment] = collect(rounded, "wide", 0)
     return jnp.stack(results)
 
 

time: 112 us -> 170 us (1.52)
  starting transfers between devices: 0.01 us -> 63.5 us
  blocking collectives: 39.5 us -> 0 us
  waiting for transfers between devices: 43.1 us -> 74.3 us
  local copies, waits for them, and re-layouts: 5.84 us -> 8.73 us
    ppermute x0 -> x30, starting transfers between devices: none -> 63.5 us  [the longest x14 62.3 us: collect(): lax.ppermute(going_down, axis, [(d, (d - 1) % ways) for d in range(ways)])]
    all_gather x2 -> x0, blocking collectives: 39.5 us -> none  [per_device(): history[moment] = lax.all_gather(rounded, 'wide', axis=0, tiled=True)]
    ppermute x0 -> x30, waiting for transfers between devices: none -> 31.6 us  [the longest x16 31.5 us: collect(): lax.ppermute(going_up, axis, [(d, (d + 1) % ways) for d in range(ways)])]
    ppermute x0 -> x30, local copies, waits for them, and re-layouts: none -> 3.3 us  [the longest x16 1.75 us: collect(): lax.ppermute(going_up, axis, [(d, (d + 1) % ways) for d in range(ways)])]
  transfers between devices with their start and end apart: 1 -> 31, of which waited for: 1 -> 17; matrix products, arithmetic and copies ran while one was open for 4% -> 5% of each run, Pallas kernels for 0% -> 0%
where the time goes in v1:
time: 170 us
  waiting for transfers between devices  74.3 us (44%)
  starting transfers between devices  63.5 us (37%)
  between operations  14.4 us (8%)
  local copies, waits for them, and re-layouts  8.73 us (5%)
  matrix products  7.02 us (4%)
  other arithmetic  2.02 us (1%)
    ppermute x14, starting transfers between devices, collect(): lax.ppermute(going_down, axis, [(d, (d - 1) % ways) for d in range(ways)])  62.3 us
    all_gather x1, waiting for transfers between devices, per_device(): later = lax.all_gather(later_current, 'wide', axis=1, tiled=True)  42 us
    ppermute x16, waiting for transfers between devices, collect(): lax.ppermute(going_up, axis, [(d, (d + 1) % ways) for d in range(ways)])  31.5 us
    dot_general x3, matrix products, per_device(): jnp.einsum('jspq,jspr->qr', local_tiles, chosen, preferred_element_type=j...  6.16 us
  transfers between devices with their start and end apart: 31, of which 17 were waited for; matrix products, arithmetic and copies ran while one was open for 5% of the time, Pallas kernels for 0%

profile of v1, /device:TPU:0, one launch (start us, length us, event | category | flops | bytes accessed | tf_op | source)
XLA Modules:
  0.0 170.0 jit_solution(2720414576977639138)
XLA Ops:
  8.3 1.9 %sort.17 = (s32[16]{0:T(128)}, s32[16]{0:T(128)S(1)}) sort(s32[16]{0:T(128)} %param.8, s32[16]{0:T(128)S(1)} %iota.4), dimensions={0}, to_apply=%region_0.0 | sort | flops 64 | bytes 256 | tf_op jit(solution)/shard_map/jit(argsort)/sort | solution.py:28
  11.7 42.0 %all-gather.2.cloned.1.call-done = bf16[4,2048,128]{2,1,0:T(8,128)(2,1)} async-done(((bf16[4,128,128]{2,1,0:T(8,128)(2,1)}), bf16[4,2048,128]{2,1,0:T(8,128)(2,1)}) %all-gather.2.cloned.1.call-update) | async-done | bytes 2097168 | tf_op jit(solution)/shard_map/all_gather | solution.py:33
  53.7 1.7 fusion.52
  55.4 1.9 %fusion = f32[128,128]{1,0:T(8,128)S(1)} fusion(pred[16,2]{1,0:T(8,128)(4,1)S(1)} %get-tuple-element.14, pred[16,2]{1,0:T(8,128)(4,1)S(1)} %get-tuple-element.13, pred[16,2]{1,0:T(8,128)(4,1)S(1)} %get-tuple-element.12, pred[16,2]{1,0:T(8,128)(4,1)S(1)} %get-tuple-element.11, bf16[16,128,128]{2,1,0:T(8,128)(2,1)S(1)} %bitcast.69, ...), kind=kOutput, calls=%fused_computation.6 | convolution fusion | flops 136855552 | bytes 3276944 | tf_op jit(solution)/shard_map/jspq,jspr->qr/dot_general | solution.py:43
  58.1 4.2 %collective-permute-start.1 = (bf16[1,128,128]{1,2,0:T(8,128)(2,1)S(1)}, bf16[1,128,128]{1,2,0:T(8,128)(2,1)S(1)}, u32[]{:S(2)}, u32[]{:S(2)}) collective-permute-start(bf16[1,128,128]{1,2,0:T(8,128)(2,1)S(1)} %fusion.47), channel_id=1, source_target_pairs={{0,15},{1,0},{2,1},{3,2},{4,3},{5,4},{6,5},{7,6},{8,7},{9,8},{10,9... | collective-permute-start | bytes 98312 | tf_op jit(solution)/shard_map/ppermute | solution.py:16
  62.4 1.5 collective-permute-done
  64.2 4.5 %collective-permute-start.3 = (bf16[1,128,128]{1,2,0:T(8,128)(2,1)S(1)}, bf16[1,128,128]{1,2,0:T(8,128)(2,1)S(1)}, u32[]{:S(2)}, u32[]{:S(2)}) collective-permute-start(bf16[1,128,128]{1,2,0:T(8,128)(2,1)S(1)} %collective-permute-done.1), channel_id=1, source_target_pairs={{0,15},{1,0},{2,1},{3,2},{4,3},{5,4},{6,5},{7,6},{8,7},{9,8},{10,9... | collective-permute-start | bytes 98312 | tf_op jit(solution)/shard_map/ppermute | solution.py:16
  68.7 1.4 collective-permute-done.2
  70.4 4.5 %collective-permute-start.5 = (bf16[1,128,128]{1,2,0:T(8,128)(2,1)S(1)}, bf16[1,128,128]{1,2,0:T(8,128)(2,1)S(1)}, u32[]{:S(2)}, u32[]{:S(2)}) collective-permute-start(bf16[1,128,128]{1,2,0:T(8,128)(2,1)S(1)} %collective-permute-done.3), channel_id=1, source_target_pairs={{0,15},{1,0},{2,1},{3,2},{4,3},{5,4},{6,5},{7,6},{8,7},{9,8},{10,9... | collective-permute-start | bytes 98312 | tf_op jit(solution)/shard_map/ppermute | solution.py:16
  74.9 1.4 collective-permute-done.4
  76.7 4.5 %collective-permute-start.7 = (bf16[1,128,128]{1,2,0:T(8,128)(2,1)S(1)}, bf16[1,128,128]{1,2,0:T(8,128)(2,1)S(1)}, u32[]{:S(2)}, u32[]{:S(2)}) collective-permute-start(bf16[1,128,128]{1,2,0:T(8,128)(2,1)S(1)} %collective-permute-done.5), channel_id=1, source_target_pairs={{0,15},{1,0},{2,1},{3,2},{4,3},{5,4},{6,5},{7,6},{8,7},{9,8},{10,9... | collective-permute-start | bytes 98312 | tf_op jit(solution)/shard_map/ppermute | solution.py:16
  81.1 1.4 collective-permute-done.6
  82.9 4.5 %collective-permute-start.9 = (bf16[1,128,128]{1,2,0:T(8,128)(2,1)S(1)}, bf16[1,128,128]{1,2,0:T(8,128)(2,1)S(1)}, u32[]{:S(2)}, u32[]{:S(2)}) collective-permute-start(bf16[1,128,128]{1,2,0:T(8,128)(2,1)S(1)} %collective-permute-done.7), channel_id=1, source_target_pairs={{0,15},{1,0},{2,1},{3,2},{4,3},{5,4},{6,5},{7,6},{8,7},{9,8},{10,9... | collective-permute-start | bytes 98312 | tf_op jit(solution)/shard_map/ppermute | solution.py:16
  87.4 1.4 collective-permute-done.8
  89.1 4.5 %collective-permute-start.11 = (bf16[1,128,128]{1,2,0:T(8,128)(2,1)S(1)}, bf16[1,128,128]{1,2,0:T(8,128)(2,1)S(1)}, u32[]{:S(2)}, u32[]{:S(2)}) collective-permute-start(bf16[1,128,128]{1,2,0:T(8,128)(2,1)S(1)} %collective-permute-done.9), channel_id=1, source_target_pairs={{0,15},{1,0},{2,1},{3,2},{4,3},{5,4},{6,5},{7,6},{8,7},{9,8},{10,9... | collective-permute-start | bytes 98312 | tf_op jit(solution)/shard_map/ppermute | solution.py:16
  95.3 4.5 %collective-permute-start.13 = (bf16[1,128,128]{1,2,0:T(8,128)(2,1)S(1)}, bf16[1,128,128]{1,2,0:T(8,128)(2,1)S(1)}, u32[]{:S(2)}, u32[]{:S(2)}) collective-permute-start(bf16[1,128,128]{1,2,0:T(8,128)(2,1)S(1)} %collective-permute-done.11), channel_id=1, source_target_pairs={{0,15},{1,0},{2,1},{3,2},{4,3},{5,4},{6,5},{7,6},{8,7},{9,8},{10,9... | collective-permute-start | bytes 98312 | tf_op jit(solution)/shard_map/ppermute | solution.py:16
  101.6 5.9 %collective-permute-done.14 = bf16[1,128,128]{1,2,0:T(8,128)(2,1)S(1)} collective-permute-done((bf16[1,128,128]{1,2,0:T(8,128)(2,1)S(1)}, bf16[1,128,128]{1,2,0:T(8,128)(2,1)S(1)}, u32[]{:S(2)}, u32[]{:S(2)}) %collective-permute-start.14) | collective-permute-done | bytes 32800 | tf_op jit(solution)/shard_map/ppermute | solution.py:13
  107.6 2.1 %fusion.1 = f32[128,128]{1,0:T(8,128)S(1)} fusion(pred[16,2]{1,0:T(8,128)(4,1)S(1)} %get-tuple-element.14, pred[16,2]{1,0:T(8,128)(4,1)S(1)} %get-tuple-element.13, pred[16,2]{1,0:T(8,128)(4,1)S(1)} %get-tuple-element.12, pred[16,2]{1,0:T(8,128)(4,1)S(1)} %get-tuple-element.11, bf16[16,128,128]{2,1,0:T(8,128)(2,1)S(1)} %constant_dynamic-update-slice_fusion.16, ...), kind=kOutput, calls=%fused_computation.7 | convolution fusion | flops 136855552 | bytes 3276944 | tf_op jit(solution)/shard_map/jspq,jspr->qr/dot_general | solution.py:43
  110.2 4.4 %collective-permute-start.16 = (bf16[1,128,128]{1,2,0:T(8,128)(2,1)S(1)}, bf16[1,128,128]{1,2,0:T(8,128)(2,1)S(1)}, u32[]{:S(2)}, u32[]{:S(2)}) collective-permute-start(bf16[1,128,128]{1,2,0:T(8,128)(2,1)S(1)} %fusion.48), channel_id=1, source_target_pairs={{0,15},{1,0},{2,1},{3,2},{4,3},{5,4},{6,5},{7,6},{8,7},{9,8},{10,9... | collective-permute-start | bytes 98312 | tf_op jit(solution)/shard_map/ppermute | solution.py:16
  114.8 1.5 collective-permute-done.15
  116.6 4.5 %collective-permute-start.18 = (bf16[1,128,128]{1,2,0:T(8,128)(2,1)S(1)}, bf16[1,128,128]{1,2,0:T(8,128)(2,1)S(1)}, u32[]{:S(2)}, u32[]{:S(2)}) collective-permute-start(bf16[1,128,128]{1,2,0:T(8,128)(2,1)S(1)} %collective-permute-done.16), channel_id=1, source_target_pairs={{0,15},{1,0},{2,1},{3,2},{4,3},{5,4},{6,5},{7,6},{8,7},{9,8},{10,9... | collective-permute-start | bytes 98312 | tf_op jit(solution)/shard_map/ppermute | solution.py:16
  121.0 1.4 collective-permute-done.17
  122.8 4.5 %collective-permute-start.20 = (bf16[1,128,128]{1,2,0:T(8,128)(2,1)S(1)}, bf16[1,128,128]{1,2,0:T(8,128)(2,1)S(1)}, u32[]{:S(2)}, u32[]{:S(2)}) collective-permute-start(bf16[1,128,128]{1,2,0:T(8,128)(2,1)S(1)} %collective-permute-done.18), channel_id=1, source_target_pairs={{0,15},{1,0},{2,1},{3,2},{4,3},{5,4},{6,5},{7,6},{8,7},{9,8},{10,9... | collective-permute-start | bytes 98312 | tf_op jit(solution)/shard_map/ppermute | solution.py:16
  127.3 1.4 collective-permute-done.19
  129.0 4.5 %collective-permute-start.22 = (bf16[1,128,128]{1,2,0:T(8,128)(2,1)S(1)}, bf16[1,128,128]{1,2,0:T(8,128)(2,1)S(1)}, u32[]{:S(2)}, u32[]{:S(2)}) collective-permute-start(bf16[1,128,128]{1,2,0:T(8,128)(2,1)S(1)} %collective-permute-done.20), channel_id=1, source_target_pairs={{0,15},{1,0},{2,1},{3,2},{4,3},{5,4},{6,5},{7,6},{8,7},{9,8},{10,9... | collective-permute-start | bytes 98312 | tf_op jit(solution)/shard_map/ppermute | solution.py:16
  133.5 1.4 collective-permute-done.21
  135.2 4.5 %collective-permute-start.24 = (bf16[1,128,128]{1,2,0:T(8,128)(2,1)S(1)}, bf16[1,128,128]{1,2,0:T(8,128)(2,1)S(1)}, u32[]{:S(2)}, u32[]{:S(2)}) collective-permute-start(bf16[1,128,128]{1,2,0:T(8,128)(2,1)S(1)} %collective-permute-done.22), channel_id=1, source_target_pairs={{0,15},{1,0},{2,1},{3,2},{4,3},{5,4},{6,5},{7,6},{8,7},{9,8},{10,9... | collective-permute-start | bytes 98312 | tf_op jit(solution)/shard_map/ppermute | solution.py:16
  139.7 1.4 collective-permute-done.23
  141.5 4.5 %collective-permute-start.26 = (bf16[1,128,128]{1,2,0:T(8,128)(2,1)S(1)}, bf16[1,128,128]{1,2,0:T(8,128)(2,1)S(1)}, u32[]{:S(2)}, u32[]{:S(2)}) collective-permute-start(bf16[1,128,128]{1,2,0:T(8,128)(2,1)S(1)} %collective-permute-done.24), channel_id=1, source_target_pairs={{0,15},{1,0},{2,1},{3,2},{4,3},{5,4},{6,5},{7,6},{8,7},{9,8},{10,9... | collective-permute-start | bytes 98312 | tf_op jit(solution)/shard_map/ppermute | solution.py:16
  147.7 4.5 %collective-permute-start.28 = (bf16[1,128,128]{1,2,0:T(8,128)(2,1)S(1)}, bf16[1,128,128]{1,2,0:T(8,128)(2,1)S(1)}, u32[]{:S(2)}, u32[]{:S(2)}) collective-permute-start(bf16[1,128,128]{1,2,0:T(8,128)(2,1)S(1)} %collective-permute-done.26), channel_id=1, source_target_pairs={{0,15},{1,0},{2,1},{3,2},{4,3},{5,4},{6,5},{7,6},{8,7},{9,8},{10,9... | collective-permute-start | bytes 98312 | tf_op jit(solution)/shard_map/ppermute | solution.py:16
  153.9 5.9 %collective-permute-done.29 = bf16[1,128,128]{1,2,0:T(8,128)(2,1)S(1)} collective-permute-done((bf16[1,128,128]{1,2,0:T(8,128)(2,1)S(1)}, bf16[1,128,128]{1,2,0:T(8,128)(2,1)S(1)}, u32[]{:S(2)}, u32[]{:S(2)}) %collective-permute-start.29) | collective-permute-done | bytes 32800 | tf_op jit(solution)/shard_map/ppermute | solution.py:13
  159.9 2.1 %fusion.2 = f32[128,128]{1,0:T(8,128)S(1)} fusion(pred[16,2]{1,0:T(8,128)(4,1)S(1)} %get-tuple-element.14, pred[16,2]{1,0:T(8,128)(4,1)S(1)} %get-tuple-element.13, pred[16,2]{1,0:T(8,128)(4,1)S(1)} %get-tuple-element.12, pred[16,2]{1,0:T(8,128)(4,1)S(1)} %get-tuple-element.11, bf16[16,128,128]{2,1,0:T(8,128)(2,1)S(1)} %constant_dynamic-update-slice_fusion, ...), kind=kOutput, calls=%fused_computation.8 | convolution fusion | flops 136855552 | bytes 3276944 | tf_op jit(solution)/shard_map/jspq,jspr->qr/dot_general | solution.py:43
  (127 shorter events, 15.6 us)
Async XLA Ops:
  6.5 47.2 %all-gather.2.cloned.1.call-start = ((), (), s32[]{:S(2)}) async-start(), calls=%async_computation | async-start | bytes 2228224 | tf_op jit(solution)/shard_map/all_gather | solution.py:33
  55.4 52.2 %copy-start.2 = (bf16[1,2048,128]{2,1,0:T(8,128)(2,1)}, bf16[1,2048,128]{2,1,0:T(8,128)(2,1)S(1)}, u32[]{:S(2)}) copy-start(bf16[1,2048,128]{2,1,0:T(8,128)(2,1)S(1)} %get-tuple-element.7) | copy-start | bytes 1572868
  57.8 6.1 %collective-permute-start = (bf16[1,128,128]{1,2,0:T(8,128)(2,1)S(1)}, bf16[1,128,128]{1,2,0:T(8,128)(2,1)S(1)}, u32[]{:S(2)}, u32[]{:S(2)}) collective-permute-start(bf16[1,128,128]{1,2,0:T(8,128)(2,1)S(1)} %fusion.47), channel_id=1, source_target_pairs={{0,1},{1,2},{2,3},{3,4},{4,5},{5,6},{6,7},{7,8},{8,9},{9,10},{10,1... | collective-permute-start | bytes 98312 | tf_op jit(solution)/shard_map/ppermute | solution.py:13
  58.1 6.0 %collective-permute-start.1 = (bf16[1,128,128]{1,2,0:T(8,128)(2,1)S(1)}, bf16[1,128,128]{1,2,0:T(8,128)(2,1)S(1)}, u32[]{:S(2)}, u32[]{:S(2)}) collective-permute-start(bf16[1,128,128]{1,2,0:T(8,128)(2,1)S(1)} %fusion.47), channel_id=1, source_target_pairs={{0,15},{1,0},{2,1},{3,2},{4,3},{5,4},{6,5},{7,6},{8,7},{9,8},{10,9... | collective-permute-start | bytes 98312 | tf_op jit(solution)/shard_map/ppermute | solution.py:16
  64.0 6.1 %collective-permute-start.2 = (bf16[1,128,128]{1,2,0:T(8,128)(2,1)S(1)}, bf16[1,128,128]{1,2,0:T(8,128)(2,1)S(1)}, u32[]{:S(2)}, u32[]{:S(2)}) collective-permute-start(bf16[1,128,128]{1,2,0:T(8,128)(2,1)S(1)} %collective-permute-done), channel_id=1, source_target_pairs={{0,1},{1,2},{2,3},{3,4},{4,5},{5,6},{6,7},{7,8},{8,9},{9,10},{10,1... | collective-permute-start | bytes 98312 | tf_op jit(solution)/shard_map/ppermute | solution.py:13
  64.2 6.1 %collective-permute-start.3 = (bf16[1,128,128]{1,2,0:T(8,128)(2,1)S(1)}, bf16[1,128,128]{1,2,0:T(8,128)(2,1)S(1)}, u32[]{:S(2)}, u32[]{:S(2)}) collective-permute-start(bf16[1,128,128]{1,2,0:T(8,128)(2,1)S(1)} %collective-permute-done.1), channel_id=1, source_target_pairs={{0,15},{1,0},{2,1},{3,2},{4,3},{5,4},{6,5},{7,6},{8,7},{9,8},{10,9... | collective-permute-start | bytes 98312 | tf_op jit(solution)/shard_map/ppermute | solution.py:16
  70.2 6.1 %collective-permute-start.4 = (bf16[1,128,128]{1,2,0:T(8,128)(2,1)S(1)}, bf16[1,128,128]{1,2,0:T(8,128)(2,1)S(1)}, u32[]{:S(2)}, u32[]{:S(2)}) collective-permute-start(bf16[1,128,128]{1,2,0:T(8,128)(2,1)S(1)} %collective-permute-done.2), channel_id=1, source_target_pairs={{0,1},{1,2},{2,3},{3,4},{4,5},{5,6},{6,7},{7,8},{8,9},{9,10},{10,1... | collective-permute-start | bytes 98312 | tf_op jit(solution)/shard_map/ppermute | solution.py:13
  70.4 6.1 %collective-permute-start.5 = (bf16[1,128,128]{1,2,0:T(8,128)(2,1)S(1)}, bf16[1,128,128]{1,2,0:T(8,128)(2,1)S(1)}, u32[]{:S(2)}, u32[]{:S(2)}) collective-permute-start(bf16[1,128,128]{1,2,0:T(8,128)(2,1)S(1)} %collective-permute-done.3), channel_id=1, source_target_pairs={{0,15},{1,0},{2,1},{3,2},{4,3},{5,4},{6,5},{7,6},{8,7},{9,8},{10,9... | collective-permute-start | bytes 98312 | tf_op jit(solution)/shard_map/ppermute | solution.py:16
  76.5 6.1 %collective-permute-start.6 = (bf16[1,128,128]{1,2,0:T(8,128)(2,1)S(1)}, bf16[1,128,128]{1,2,0:T(8,128)(2,1)S(1)}, u32[]{:S(2)}, u32[]{:S(2)}) collective-permute-start(bf16[1,128,128]{1,2,0:T(8,128)(2,1)S(1)} %collective-permute-done.4), channel_id=1, source_target_pairs={{0,1},{1,2},{2,3},{3,4},{4,5},{5,6},{6,7},{7,8},{8,9},{9,10},{10,1... | collective-permute-start | bytes 98312 | tf_op jit(solution)/shard_map/ppermute | solution.py:13
  76.7 6.1 %collective-permute-start.7 = (bf16[1,128,128]{1,2,0:T(8,128)(2,1)S(1)}, bf16[1,128,128]{1,2,0:T(8,128)(2,1)S(1)}, u32[]{:S(2)}, u32[]{:S(2)}) collective-permute-start(bf16[1,128,128]{1,2,0:T(8,128)(2,1)S(1)} %collective-permute-done.5), channel_id=1, source_target_pairs={{0,15},{1,0},{2,1},{3,2},{4,3},{5,4},{6,5},{7,6},{8,7},{9,8},{10,9... | collective-permute-start | bytes 98312 | tf_op jit(solution)/shard_map/ppermute | solution.py:16
  82.7 6.1 %collective-permute-start.8 = (bf16[1,128,128]{1,2,0:T(8,128)(2,1)S(1)}, bf16[1,128,128]{1,2,0:T(8,128)(2,1)S(1)}, u32[]{:S(2)}, u32[]{:S(2)}) collective-permute-start(bf16[1,128,128]{1,2,0:T(8,128)(2,1)S(1)} %collective-permute-done.6), channel_id=1, source_target_pairs={{0,1},{1,2},{2,3},{3,4},{4,5},{5,6},{6,7},{7,8},{8,9},{9,10},{10,1... | collective-permute-start | bytes 98312 | tf_op jit(solution)/shard_map/ppermute | solution.py:13
  82.9 6.1 %collective-permute-start.9 = (bf16[1,128,128]{1,2,0:T(8,128)(2,1)S(1)}, bf16[1,128,128]{1,2,0:T(8,128)(2,1)S(1)}, u32[]{:S(2)}, u32[]{:S(2)}) collective-permute-start(bf16[1,128,128]{1,2,0:T(8,128)(2,1)S(1)} %collective-permute-done.7), channel_id=1, source_target_pairs={{0,15},{1,0},{2,1},{3,2},{4,3},{5,4},{6,5},{7,6},{8,7},{9,8},{10,9... | collective-permute-start | bytes 98312 | tf_op jit(solution)/shard_map/ppermute | solution.py:16
  88.9 6.1 %collective-permute-start.10 = (bf16[1,128,128]{1,2,0:T(8,128)(2,1)S(1)}, bf16[1,128,128]{1,2,0:T(8,128)(2,1)S(1)}, u32[]{:S(2)}, u32[]{:S(2)}) collective-permute-start(bf16[1,128,128]{1,2,0:T(8,128)(2,1)S(1)} %collective-permute-done.8), channel_id=1, source_target_pairs={{0,1},{1,2},{2,3},{3,4},{4,5},{5,6},{6,7},{7,8},{8,9},{9,10},{10,1... | collective-permute-start | bytes 98312 | tf_op jit(solution)/shard_map/ppermute | solution.py:13
  89.1 6.1 %collective-permute-start.11 = (bf16[1,128,128]{1,2,0:T(8,128)(2,1)S(1)}, bf16[1,128,128]{1,2,0:T(8,128)(2,1)S(1)}, u32[]{:S(2)}, u32[]{:S(2)}) collective-permute-start(bf16[1,128,128]{1,2,0:T(8,128)(2,1)S(1)} %collective-permute-done.9), channel_id=1, source_target_pairs={{0,15},{1,0},{2,1},{3,2},{4,3},{5,4},{6,5},{7,6},{8,7},{9,8},{10,9... | collective-permute-start | bytes 98312 | tf_op jit(solution)/shard_map/ppermute | solution.py:16
  95.1 6.1 %collective-permute-start.12 = (bf16[1,128,128]{1,2,0:T(8,128)(2,1)S(1)}, bf16[1,128,128]{1,2,0:T(8,128)(2,1)S(1)}, u32[]{:S(2)}, u32[]{:S(2)}) collective-permute-start(bf16[1,128,128]{1,2,0:T(8,128)(2,1)S(1)} %collective-permute-done.10), channel_id=1, source_target_pairs={{0,1},{1,2},{2,3},{3,4},{4,5},{5,6},{6,7},{7,8},{8,9},{9,10},{10,1... | collective-permute-start | bytes 98312 | tf_op jit(solution)/shard_map/ppermute | solution.py:13
  95.3 6.1 %collective-permute-start.13 = (bf16[1,128,128]{1,2,0:T(8,128)(2,1)S(1)}, bf16[1,128,128]{1,2,0:T(8,128)(2,1)S(1)}, u32[]{:S(2)}, u32[]{:S(2)}) collective-permute-start(bf16[1,128,128]{1,2,0:T(8,128)(2,1)S(1)} %collective-permute-done.11), channel_id=1, source_target_pairs={{0,15},{1,0},{2,1},{3,2},{4,3},{5,4},{6,5},{7,6},{8,7},{9,8},{10,9... | collective-permute-start | bytes 98312 | tf_op jit(solution)/shard_map/ppermute | solution.py:16
  101.4 6.1 %collective-permute-start.14 = (bf16[1,128,128]{1,2,0:T(8,128)(2,1)S(1)}, bf16[1,128,128]{1,2,0:T(8,128)(2,1)S(1)}, u32[]{:S(2)}, u32[]{:S(2)}) collective-permute-start(bf16[1,128,128]{1,2,0:T(8,128)(2,1)S(1)} %collective-permute-done.12), channel_id=1, source_target_pairs={{0,1},{1,2},{2,3},{3,4},{4,5},{5,6},{6,7},{7,8},{8,9},{9,10},{10,1... | collective-permute-start | bytes 98312 | tf_op jit(solution)/shard_map/ppermute | solution.py:13
  110.1 6.1 %collective-permute-start.15 = (bf16[1,128,128]{1,2,0:T(8,128)(2,1)S(1)}, bf16[1,128,128]{1,2,0:T(8,128)(2,1)S(1)}, u32[]{:S(2)}, u32[]{:S(2)}) collective-permute-start(bf16[1,128,128]{1,2,0:T(8,128)(2,1)S(1)} %fusion.48), channel_id=1, source_target_pairs={{0,1},{1,2},{2,3},{3,4},{4,5},{5,6},{6,7},{7,8},{8,9},{9,10},{10,1... | collective-permute-start | bytes 98312 | tf_op jit(solution)/shard_map/ppermute | solution.py:13
  110.2 6.2 %collective-permute-start.16 = (bf16[1,128,128]{1,2,0:T(8,128)(2,1)S(1)}, bf16[1,128,128]{1,2,0:T(8,128)(2,1)S(1)}, u32[]{:S(2)}, u32[]{:S(2)}) collective-permute-start(bf16[1,128,128]{1,2,0:T(8,128)(2,1)S(1)} %fusion.48), channel_id=1, source_target_pairs={{0,15},{1,0},{2,1},{3,2},{4,3},{5,4},{6,5},{7,6},{8,7},{9,8},{10,9... | collective-permute-start | bytes 98312 | tf_op jit(solution)/shard_map/ppermute | solution.py:16
  116.4 6.1 %collective-permute-start.17 = (bf16[1,128,128]{1,2,0:T(8,128)(2,1)S(1)}, bf16[1,128,128]{1,2,0:T(8,128)(2,1)S(1)}, u32[]{:S(2)}, u32[]{:S(2)}) collective-permute-start(bf16[1,128,128]{1,2,0:T(8,128)(2,1)S(1)} %collective-permute-done.15), channel_id=1, source_target_pairs={{0,1},{1,2},{2,3},{3,4},{4,5},{5,6},{6,7},{7,8},{8,9},{9,10},{10,1... | collective-permute-start | bytes 98312 | tf_op jit(solution)/shard_map/ppermute | solution.py:13
  116.6 6.1 %collective-permute-start.18 = (bf16[1,128,128]{1,2,0:T(8,128)(2,1)S(1)}, bf16[1,128,128]{1,2,0:T(8,128)(2,1)S(1)}, u32[]{:S(2)}, u32[]{:S(2)}) collective-permute-start(bf16[1,128,128]{1,2,0:T(8,128)(2,1)S(1)} %collective-permute-done.16), channel_id=1, source_target_pairs={{0,15},{1,0},{2,1},{3,2},{4,3},{5,4},{6,5},{7,6},{8,7},{9,8},{10,9... | collective-permute-start | bytes 98312 | tf_op jit(solution)/shard_map/ppermute | solution.py:16
  122.6 6.1 %collective-permute-start.19 = (bf16[1,128,128]{1,2,0:T(8,128)(2,1)S(1)}, bf16[1,128,128]{1,2,0:T(8,128)(2,1)S(1)}, u32[]{:S(2)}, u32[]{:S(2)}) collective-permute-start(bf16[1,128,128]{1,2,0:T(8,128)(2,1)S(1)} %collective-permute-done.17), channel_id=1, source_target_pairs={{0,1},{1,2},{2,3},{3,4},{4,5},{5,6},{6,7},{7,8},{8,9},{9,10},{10,1... | collective-permute-start | bytes 98312 | tf_op jit(solution)/shard_map/ppermute | solution.py:13
  122.8 6.1 %collective-permute-start.20 = (bf16[1,128,128]{1,2,0:T(8,128)(2,1)S(1)}, bf16[1,128,128]{1,2,0:T(8,128)(2,1)S(1)}, u32[]{:S(2)}, u32[]{:S(2)}) collective-permute-start(bf16[1,128,128]{1,2,0:T(8,128)(2,1)S(1)} %collective-permute-done.18), channel_id=1, source_target_pairs={{0,15},{1,0},{2,1},{3,2},{4,3},{5,4},{6,5},{7,6},{8,7},{9,8},{10,9... | collective-permute-start | bytes 98312 | tf_op jit(solution)/shard_map/ppermute | solution.py:16
  128.8 6.1 %collective-permute-start.21 = (bf16[1,128,128]{1,2,0:T(8,128)(2,1)S(1)}, bf16[1,128,128]{1,2,0:T(8,128)(2,1)S(1)}, u32[]{:S(2)}, u32[]{:S(2)}) collective-permute-start(bf16[1,128,128]{1,2,0:T(8,128)(2,1)S(1)} %collective-permute-done.19), channel_id=1, source_target_pairs={{0,1},{1,2},{2,3},{3,4},{4,5},{5,6},{6,7},{7,8},{8,9},{9,10},{10,1... | collective-permute-start | bytes 98312 | tf_op jit(solution)/shard_map/ppermute | solution.py:13
  129.0 6.1 %collective-permute-start.22 = (bf16[1,128,128]{1,2,0:T(8,128)(2,1)S(1)}, bf16[1,128,128]{1,2,0:T(8,128)(2,1)S(1)}, u32[]{:S(2)}, u32[]{:S(2)}) collective-permute-start(bf16[1,128,128]{1,2,0:T(8,128)(2,1)S(1)} %collective-permute-done.20), channel_id=1, source_target_pairs={{0,15},{1,0},{2,1},{3,2},{4,3},{5,4},{6,5},{7,6},{8,7},{9,8},{10,9... | collective-permute-start | bytes 98312 | tf_op jit(solution)/shard_map/ppermute | solution.py:16
  135.0 6.1 %collective-permute-start.23 = (bf16[1,128,128]{1,2,0:T(8,128)(2,1)S(1)}, bf16[1,128,128]{1,2,0:T(8,128)(2,1)S(1)}, u32[]{:S(2)}, u32[]{:S(2)}) collective-permute-start(bf16[1,128,128]{1,2,0:T(8,128)(2,1)S(1)} %collective-permute-done.21), channel_id=1, source_target_pairs={{0,1},{1,2},{2,3},{3,4},{4,5},{5,6},{6,7},{7,8},{8,9},{9,10},{10,1... | collective-permute-start | bytes 98312 | tf_op jit(solution)/shard_map/ppermute | solution.py:13
  135.2 6.1 %collective-permute-start.24 = (bf16[1,128,128]{1,2,0:T(8,128)(2,1)S(1)}, bf16[1,128,128]{1,2,0:T(8,128)(2,1)S(1)}, u32[]{:S(2)}, u32[]{:S(2)}) collective-permute-start(bf16[1,128,128]{1,2,0:T(8,128)(2,1)S(1)} %collective-permute-done.22), channel_id=1, source_target_pairs={{0,15},{1,0},{2,1},{3,2},{4,3},{5,4},{6,5},{7,6},{8,7},{9,8},{10,9... | collective-permute-start | bytes 98312 | tf_op jit(solution)/shard_map/ppermute | solution.py:16
  141.3 6.1 %collective-permute-start.25 = (bf16[1,128,128]{1,2,0:T(8,128)(2,1)S(1)}, bf16[1,128,128]{1,2,0:T(8,128)(2,1)S(1)}, u32[]{:S(2)}, u32[]{:S(2)}) collective-permute-start(bf16[1,128,128]{1,2,0:T(8,128)(2,1)S(1)} %collective-permute-done.23), channel_id=1, source_target_pairs={{0,1},{1,2},{2,3},{3,4},{4,5},{5,6},{6,7},{7,8},{8,9},{9,10},{10,1... | collective-permute-start | bytes 98312 | tf_op jit(solution)/shard_map/ppermute | solution.py:13
  141.5 6.1 %collective-permute-start.26 = (bf16[1,128,128]{1,2,0:T(8,128)(2,1)S(1)}, bf16[1,128,128]{1,2,0:T(8,128)(2,1)S(1)}, u32[]{:S(2)}, u32[]{:S(2)}) collective-permute-start(bf16[1,128,128]{1,2,0:T(8,128)(2,1)S(1)} %collective-permute-done.24), channel_id=1, source_target_pairs={{0,15},{1,0},{2,1},{3,2},{4,3},{5,4},{6,5},{7,6},{8,7},{9,8},{10,9... | collective-permute-start | bytes 98312 | tf_op jit(solution)/shard_map/ppermute | solution.py:16
  147.5 6.1 %collective-permute-start.27 = (bf16[1,128,128]{1,2,0:T(8,128)(2,1)S(1)}, bf16[1,128,128]{1,2,0:T(8,128)(2,1)S(1)}, u32[]{:S(2)}, u32[]{:S(2)}) collective-permute-start(bf16[1,128,128]{1,2,0:T(8,128)(2,1)S(1)} %collective-permute-done.25), channel_id=1, source_target_pairs={{0,1},{1,2},{2,3},{3,4},{4,5},{5,6},{6,7},{7,8},{8,9},{9,10},{10,1... | collective-permute-start | bytes 98312 | tf_op jit(solution)/shard_map/ppermute | solution.py:13
  147.7 6.1 %collective-permute-start.28 = (bf16[1,128,128]{1,2,0:T(8,128)(2,1)S(1)}, bf16[1,128,128]{1,2,0:T(8,128)(2,1)S(1)}, u32[]{:S(2)}, u32[]{:S(2)}) collective-permute-start(bf16[1,128,128]{1,2,0:T(8,128)(2,1)S(1)} %collective-permute-done.26), channel_id=1, source_target_pairs={{0,15},{1,0},{2,1},{3,2},{4,3},{5,4},{6,5},{7,6},{8,7},{9,8},{10,9... | collective-permute-start | bytes 98312 | tf_op jit(solution)/shard_map/ppermute | solution.py:16
  153.7 6.1 %collective-permute-start.29 = (bf16[1,128,128]{1,2,0:T(8,128)(2,1)S(1)}, bf16[1,128,128]{1,2,0:T(8,128)(2,1)S(1)}, u32[]{:S(2)}, u32[]{:S(2)}) collective-permute-start(bf16[1,128,128]{1,2,0:T(8,128)(2,1)S(1)} %collective-permute-done.27), channel_id=1, source_target_pairs={{0,1},{1,2},{2,3},{3,4},{4,5},{5,6},{6,7},{7,8},{8,9},{9,10},{10,1... | collective-permute-start | bytes 98312 | tf_op jit(solution)/shard_map/ppermute | solution.py:13
  (4 other events, 10.1 us)
Sparse Core Ops, SparseCore 0:
  9.5 44.1 all-gather.1
